TPU v7x, 32 devices: a whole 2x2x4 slice. The times are simulated.
32 devices in a mesh: front: 8 (over z, x), grp: 4 (over y, core).
Axes of the slice: x: 2, y: 2, z: 4, core: 2. Of those that a mesh axis runs over, the one named last changes fastest.
Arguments:
- front_block: float32 [8, 16384, 1408], P('front', 'grp'), as said below
- child_blocks: float32 [8, 4, 4, 16, 1408], P('front', 'grp'), may hold values from -0.5 to 0.5
- child_rows: int32 [8, 4, 4, 16], P('front', 'grp'), may hold values from 0 to 4095
- child_dest: int32 [8, 4, 4, 1], P('front', 'grp'), may hold values from 0 to 7; in each aligned block of 4 rows (0 to 3, 4 to 7, ..., all dimensions but the last counted through in order) at most 2 rows name the same one
- panel_owner: int32 [8], P('front'), may hold values from 0 to 3
Outputs:
- panel_factor: float32 [8, 16384, 512], P('front', 'grp')
- schur_block: float32 [8, 16384, 896], P('front', 'grp')
Inputs may be any that keep to these rules, and one draw needn't show every extreme that they name: `child_dest`: among the 4 blocks of one device no front is named more than 2 times, and in every draw some device names some front exactly 2 times. `front_block`: for every front and row block, the first 512 rows' leading 512 x 512 block has a positive diagonal that dominates; other entries lie within -2.3 to 2.3.
All inputs are finite; a program needn't handle non-finite values.
Results may differ from a plain program's by a relative error of at most 0.0003.
Values sent between devices are 32-bit elements; how exact they have to be, the bound alone decides.
No kernel may reach another device: no remote copies, remote signals or barrier semaphores. Data moves between devices by JAX's collectives and lax.ppermute only.
A program may use at most 128 MiB of HBM per device.

v0:
```python
import jax
import jax.numpy as jnp
from jax import lax
from jax.sharding import PartitionSpec as P

PB = 512
CAP = 2


def spread(array, axis, root):
    mine = lax.axis_index(axis) == root
    return lax.psum(jnp.where(mine, array, jnp.zeros_like(array)), axis)


def right_solve(factor, rows):
    return lax.linalg.triangular_solve(factor, rows, left_side=False, lower=True, transpose_a=True)


def pack_slots(values, slot_index, front_count):
    empty = jnp.zeros((front_count * CAP,) + values.shape[1:], values.dtype)
    filled = empty.at[slot_index].set(values)
    return filled.reshape((front_count, CAP) + values.shape[1:])


def local(front_block, child_blocks, child_rows, child_dest, panel_owner):
    local_rows = front_block[0]
    front_count = lax.axis_size("front")
    blocks = child_blocks[0, 0]
    row_lists = child_rows[0, 0]
    target_front = child_dest[0, 0, :, 0]
    block_count = target_front.shape[0]
    position = jnp.arange(block_count, dtype=jnp.int32)
    same_front = target_front[:, None] == target_front[None, :]
    earlier = position[None, :] < position[:, None]
    slot_index = target_front * CAP + jnp.sum((same_front & earlier).astype(jnp.int32), axis=1)
    send_rows = pack_slots(row_lists, slot_index, front_count)
    panel_cols = PB
    send_panel = pack_slots(blocks[:, :, :panel_cols], slot_index, front_count)
    got_panel, got_rows = (
        lax.all_to_all(send_panel, "front", split_axis=0, concat_axis=0, tiled=True),
        lax.all_to_all(send_rows, "front", split_axis=0, concat_axis=0, tiled=True),
    )
    flat_rows = got_rows.reshape(-1)
    panel_part = local_rows[:, :panel_cols].at[flat_rows].add(got_panel.reshape(-1, panel_cols))
    local_rows = jnp.concatenate([panel_part, local_rows[:, panel_cols:]], axis=1)
    send_trail = pack_slots(blocks[:, :, panel_cols:], slot_index, front_count)
    trailing_rows = lax.all_to_all(send_trail, "front", split_axis=0, concat_axis=0, tiled=True)
    win_cols = local_rows.shape[1] - panel_cols
    owner_index = panel_owner[0]
    is_owner = lax.axis_index("grp") == owner_index
    pivot_block = spread(local_rows[:panel_cols, :panel_cols], "grp", owner_index)
    symmetric = 0.5 * (pivot_block + pivot_block.T)
    pivot_factor = jnp.linalg.cholesky(symmetric)
    solved = right_solve(pivot_factor, local_rows[:, :panel_cols])
    window = spread(solved[panel_cols : panel_cols + win_cols], "grp", owner_index)
    schur_part = local_rows[:, panel_cols:] - jnp.dot(
        solved, window.T, precision=lax.Precision.HIGHEST
    )
    schur_part = schur_part.at[flat_rows].add(trailing_rows.reshape(-1, win_cols))
    top_rows = jnp.where(is_owner, pivot_factor, solved[:panel_cols])
    panel_rows = jnp.concatenate([top_rows, solved[panel_cols:]], axis=0)
    return (panel_rows[None], schur_part[None])


def solution(mesh):
    placed = (
        P("front", "grp", None),
        P("front", "grp", None, None, None),
        P("front", "grp", None, None),
        P("front", "grp", None, None),
        P("front"),
    )
    return jax.shard_map(
        local,
        mesh=mesh,
        in_specs=placed,
        out_specs=(P("front", "grp", None), P("front", "grp", None)),
        check_vma=False,
    )
```

profile of v0, /device:TPU:0, one launch (start us, length us, event | category | flops | bytes accessed | tf_op | source)
XLA Modules:
  0.0 376.9 jit_solution(13516703856548817198)
XLA Ops:
  7.2 0.9 convert_reduce_fusion
  8.1 0.7 fusion.38
  8.8 1.2 scatter_custom_fusion
  9.9 7.3 %all-to-all-start = ((s32[8,2,16]{2,1,0:T(2,128)}), s32[8,2,16]{2,1,0:T(2,128)S(1)}, u32[]{:S(2)}, u32[]{:S(2)}) async-start(s32[8,2,16]{2,1,0:T(2,128)} %bitcast.7), calls=%async_computation | async-start | bytes 16384 | tf_op jit(solution)/shard_map/all_to_all | solution.py:41
  17.2 0.9 slice.147
  18.1 0.9 broadcast_in_dim.31
  18.9 2.0 scatter_fusion
  21.0 2.7 all-to-all-done
  23.7 3.5 all-to-all-start.1
  27.9 7.9 %slice.146 = f32[4096,512]{1,0:T(8,128)} slice(f32[4096,1408]{1,0:T(8,128)} %bitcast.80), slice={[0:4096], [0:512]} | slice | bytes 16777216 | tf_op jit(solution)/shard_map/slice | solution.py:44
  35.9 5.0 %all-to-all-done.1 = f32[8,2,16,512]{3,2,1,0:T(8,128)S(1)} async-done(((f32[8,2,16,512]{3,2,1,0:T(8,128)}), f32[8,2,16,512]{3,2,1,0:T(8,128)S(1)}, u32[]{:S(2)}, u32[]{:S(2)}) %all-to-all-start.1) | async-done | bytes 524320 | tf_op jit(solution)/shard_map/all_to_all | solution.py:40
  40.9 9.0 %scatter_fusion.1 = f32[4096,512]{1,0:T(8,128)} fusion(f32[4096,512]{1,0:T(8,128)} %slice.146, s32[256]{0:T(256)S(1)} %bitcast.85, f32[256,512]{1,0:T(8,128)S(1)} %bitcast.82), kind=kCustom, calls=%fused_computation.2 | custom fusion | flops 131072 | bytes 1573888 | tf_op jit(solution)/shard_map/scatter-add | solution.py:44
  49.9 1.3 slice.148
  51.6 1.1 broadcast_select_fusion
  52.7 1.0 broadcast_in_dim.35
  53.7 2.2 scatter_fusion.2
  55.9 4.2 %all-to-all-start.2 = ((f32[8,2,16,896]{3,2,1,0:T(8,128)}), f32[8,2,16,896]{3,2,1,0:T(8,128)}, u32[]{:S(2)}, u32[]{:S(2)}) async-start(f32[8,2,16,896]{3,2,1,0:T(8,128)} %bitcast.25), calls=%async_computation.2 | async-start | bytes 1835008 | tf_op jit(solution)/shard_map/all_to_all | solution.py:47
  60.7 27.5 %all-reduce.4.cloned.1.call-done = f32[512,512]{0,1:T(8,128)} async-done(((f32[512,512]{0,1:T(8,128)}), f32[512,512]{0,1:T(8,128)}) %all-reduce.4.cloned.1.call-update) | async-done | bytes 1048592 | tf_op jit(solution)/shard_map/psum | solution.py:12
  88.1 1.6 copy.34
  90.6 11.7 %cholesky.103 = f32[128,128]{1,0:T(8,128)S(1)} custom-call(f32[128,128]{1,0:T(8,128)S(1)} %cholesky.263), custom_call_target="Cholesky" | custom-call | tf_op jit(solution)/shard_map/jit(cholesky)/cholesky | solution.py:53
  102.5 9.8 %custom-call.30 = f32[1,128,128]{1,2,0:T(8,128)S(1)} custom-call(f32[1,128,128]{2,1,0:T(8,128)S(1)} %get-tuple-element.43), custom_call_target="InvertDiagBlocksLowerTriangular" | custom-call | tf_op jit(solution)/shard_map/jit(cholesky)/cholesky | solution.py:53
  113.1 11.7 %cholesky.215 = f32[128,128]{1,0:T(8,128)S(1)} custom-call(f32[128,128]{1,0:T(8,128)S(1)} %cholesky.267), custom_call_target="Cholesky" | custom-call | tf_op jit(solution)/shard_map/jit(cholesky)/cholesky | solution.py:53
  125.0 9.9 %custom-call.31 = f32[1,128,128]{1,2,0:T(8,128)S(1)} custom-call(f32[1,128,128]{2,1,0:T(8,128)S(1)} %get-tuple-element.41), custom_call_target="InvertDiagBlocksLowerTriangular" | custom-call | tf_op jit(solution)/shard_map/jit(cholesky)/cholesky | solution.py:53
  135.4 1.5 convolution_subtract_fusion.3
  136.9 11.7 %cholesky.236 = f32[128,128]{1,0:T(8,128)S(1)} custom-call(f32[128,128]{1,0:T(8,128)S(1)} %cholesky.272), custom_call_target="Cholesky" | custom-call | tf_op jit(solution)/shard_map/jit(cholesky)/cholesky | solution.py:53
  148.8 9.8 %custom-call.32 = f32[1,128,128]{1,2,0:T(8,128)S(1)} custom-call(f32[1,128,128]{2,1,0:T(8,128)S(1)} %get-tuple-element.39), custom_call_target="InvertDiagBlocksLowerTriangular" | custom-call | tf_op jit(solution)/shard_map/jit(cholesky)/cholesky | solution.py:53
  158.9 1.3 convolution_subtract_fusion.4
  160.2 12.1 %cholesky.253 = f32[128,128]{1,0:T(8,128)S(1)} custom-call(f32[128,128]{1,0:T(8,128)S(1)} %convolution_subtract_fusion.4), custom_call_target="Cholesky" | custom-call | tf_op jit(solution)/shard_map/jit(cholesky)/cholesky | solution.py:53
  172.4 0.7 compare_reduce_fusion.1
  173.2 0.6 compare_reduce_fusion
  173.8 0.7 compare_reduce_fusion.2
  177.1 11.3 %while.1 = (s32[]{:T(128)}, f32[512,512]{0,1:T(8,128)S(1)}, s32[4,2]{0,1:T(2,128)S(1)}, f32[4,128,128]{2,1,0:T(8,128)}, s32[]{:T(128)}) while((s32[]{:T(128)}, f32[512,512]{0,1:T(8,128)S(1)}, s32[4,2]{0,1:T(2,128)S(1)}, f32[4,128,128]{2,1,0:T(8,128)}, s32[]{:T(128)}) %tuple.33), condition=%wide.while_cond, body=%wide.while_body.sunk | while | flops 2 | bytes 393329 | solution.py:16
  177.2 0.6 fusion.49
  177.8 1.4 dynamic-slice.7
  179.4 0.6 bitcast_dynamic-update-slice_fusion.2
  180.1 0.6 fusion.49
  180.7 1.4 dynamic-slice.7
  182.2 0.6 bitcast_dynamic-update-slice_fusion.2
  183.5 1.4 dynamic-slice.7
  185.0 0.6 bitcast_dynamic-update-slice_fusion.2
  185.7 0.6 fusion.49
  186.3 1.4 dynamic-slice.7
  187.8 0.6 bitcast_dynamic-update-slice_fusion.2
  188.5 1.0 copy-done.9
  189.4 40.1 %custom-call.33 = f32[4,128,128]{1,2,0:T(8,128)S(1)} custom-call(f32[4,128,128]{2,1,0:T(8,128)} %get-tuple-element.9), custom_call_target="InvertDiagBlocksLowerTriangular" | custom-call | tf_op jit(solution)/shard_map/triangular_solve | solution.py:16
  229.6 3.6 fusion.12
  233.2 5.2 %convolution_subtract_fusion.1 = f32[4096,128]{1,0:T(8,128)S(1)} fusion(f32[4096,128]{0,1:T(8,128)S(1)} %fusion.12, f32[4096,512]{1,0:T(8,128)} %scatter_fusion.1, f32[512,512]{0,1:T(8,128)} %copy-done.9), kind=kOutput, calls=%fused_computation.17 | convolution fusion | flops 805830656 | bytes 6356992 | tf_op jit(solution)/shard_map/triangular_solve | solution.py:16
  238.4 2.0 fusion.27
  240.4 9.8 %convolution_subtract_fusion = f32[4096,128]{1,0:T(8,128)S(1)} fusion(f32[4096,128]{0,1:T(8,128)S(1)} %fusion.27, f32[4096,128]{0,1:T(8,128)S(1)} %fusion.12, f32[4096,512]{1,0:T(8,128)} %scatter_fusion.1, f32[512,512]{0,1:T(8,128)} %copy-done.9), kind=kOutput, calls=%fused_computation.16 | convolution fusion | flops 1612185600 | bytes 8519680 | tf_op jit(solution)/shard_map/triangular_solve | solution.py:16
  250.2 2.0 fusion.26
  252.2 12.8 %fusion.6 = f32[4096,128]{1,0:T(8,128)S(1)} fusion(f32[4096,128]{0,1:T(8,128)S(1)} %fusion.26, f32[4096,128]{0,1:T(8,128)S(1)} %fusion.27, f32[4096,128]{0,1:T(8,128)S(1)} %fusion.12, f32[4096,512]{1,0:T(8,128)} %scatter_fusion.1, f32[512,512]{0,1:T(8,128)} %copy-done.9), kind=kOutput, calls=%fused_computation.18 | convolution fusion | flops 2419589120 | bytes 10682368 | tf_op jit(solution)/shard_map/triangular_solve | solution.py:16
  265.0 2.1 fusion.25
  267.1 1.3 copy-done.6
  268.5 1.5 maximum_select_fusion
  270.0 5.9 %pad_maximum_fusion = f32[4096,512]{0,1:T(8,128)} fusion(f32[4096,128]{0,1:T(8,128)} %copy-done.6, f32[4096,128]{0,1:T(8,128)} %copy-done.4, f32[4096,128]{0,1:T(8,128)} %copy-done.2, f32[4096,128]{0,1:T(8,128)S(1)} %fusion.12), kind=kLoop, calls=%fused_computation.8 | loop fusion | flops 6291456 | bytes 16777216 | tf_op jit(solution)/shard_map/triangular_solve | solution.py:16
  275.9 1.6 copy-done.3
  277.5 0.6 copy-done.5
  278.1 0.6 copy-done.7
  278.9 3.1 slice-done
  282.0 3.9 %maximum_bitcast_fusion = f32[1,4096,512]{1,2,0:T(8,128)} fusion(f32[3584,512]{0,1:T(8,128)S(1)} %slice-done, f32[512,512]{0,1:T(8,128)S(1)} %maximum_select_fusion.1), kind=kLoop, calls=%fused_computation.9 | loop fusion | flops 2097152 | bytes 16777216 | tf_op jit(solution)/shard_map/broadcast_in_dim | solution.py:62
  285.9 9.0 %copy.44 = f32[1,4096,512]{2,1,0:T(8,128)} copy(f32[1,4096,512]{1,2,0:T(8,128)} %maximum_bitcast_fusion) | data formatting | bytes 16777216
  294.9 28.4 %all-reduce.6.cloned.1.call-done = f32[896,512]{0,1:T(8,128)} async-done(((f32[896,512]{0,1:T(8,128)}), f32[896,512]{0,1:T(8,128)}) %all-reduce.6.cloned.1.call-update) | async-done | bytes 1835024 | tf_op jit(solution)/shard_map/psum | solution.py:12
  323.3 32.7 %slice_subtract_fusion = f32[4096,896]{1,0:T(8,128)} fusion(f32[4096,1408]{1,0:T(8,128)} %bitcast.81, f32[896,512]{0,1:T(8,128)} %all-reduce.6.cloned.1.call-done, f32[4096,128]{0,1:T(8,128)} %copy-done.6, f32[4096,128]{0,1:T(8,128)} %copy-done.4, f32[4096,128]{0,1:T(8,128)} %copy-done.2, f32[4096,128]{0,1:T(8,128)S(1)} %fusion.12), kind=kOutput, calls=%fused_computation.7 | convolution fusion | flops 22558539776 | bytes 39583744 | tf_op jit(solution)/shard_map/dot_general | solution.py:56
  356.0 13.9 %scatter_fusion.3 = f32[4096,896]{1,0:T(8,128)} fusion(f32[4096,896]{1,0:T(8,128)} %slice_subtract_fusion, s32[256]{0:T(256)S(1)} %bitcast.86, f32[256,896]{1,0:T(8,128)} %bitcast.26), kind=kCustom, calls=%fused_computation.4 | custom fusion | flops 229376 | bytes 2753536 | tf_op jit(solution)/shard_map/scatter-add | solution.py:59
  (67 shorter events, 5.5 us)
Async XLA Ops:
  7.2 1.6 copy-start
  9.9 13.8 %all-to-all-start = ((s32[8,2,16]{2,1,0:T(2,128)}), s32[8,2,16]{2,1,0:T(2,128)S(1)}, u32[]{:S(2)}, u32[]{:S(2)}) async-start(s32[8,2,16]{2,1,0:T(2,128)} %bitcast.7), calls=%async_computation | async-start | bytes 16384 | tf_op jit(solution)/shard_map/all_to_all | solution.py:41
  23.7 17.2 %all-to-all-start.1 = ((f32[8,2,16,512]{3,2,1,0:T(8,128)}), f32[8,2,16,512]{3,2,1,0:T(8,128)S(1)}, u32[]{:S(2)}, u32[]{:S(2)}) async-start(f32[8,2,16,512]{3,2,1,0:T(8,128)} %bitcast.10), calls=%async_computation.1 | async-start | bytes 1048576 | tf_op jit(solution)/shard_map/all_to_all | solution.py:40
  27.2 61.0 %all-reduce.4.cloned.1.call-start = ((), (), s32[]{:S(2)}) async-start(), calls=%async_computation.3 | async-start | bytes 2097152 | tf_op jit(solution)/shard_map/psum | solution.py:12
  51.6 1.1 copy-start.11
  55.9 300.1 %all-to-all-start.2 = ((f32[8,2,16,896]{3,2,1,0:T(8,128)}), f32[8,2,16,896]{3,2,1,0:T(8,128)}, u32[]{:S(2)}, u32[]{:S(2)}) async-start(f32[8,2,16,896]{3,2,1,0:T(8,128)} %bitcast.25), calls=%async_computation.2 | async-start | bytes 1835008 | tf_op jit(solution)/shard_map/all_to_all | solution.py:47
  60.1 263.2 %all-reduce.6.cloned.1.call-start = ((), (), s32[]{:S(2)}) async-start(), calls=%async_computation.4 | async-start | bytes 3670016 | tf_op jit(solution)/shard_map/psum | solution.py:12
  88.1 1.7 copy-start.8
  90.6 34.4 %copy-start.10 = (f32[512,512]{1,0:T(8,128)}, f32[512,512]{1,0:T(8,128)S(1)}, u32[]{:S(2)}) copy-start(f32[512,512]{1,0:T(8,128)S(1)} %fusion.14) | copy-start | bytes 3145732
  188.5 1.0 copy-start.9
  240.4 26.7 %copy-start.2 = (f32[4096,128]{0,1:T(8,128)}, f32[4096,128]{0,1:T(8,128)S(1)}, u32[]{:S(2)}) copy-start(f32[4096,128]{0,1:T(8,128)S(1)} %fusion.27) | copy-start | bytes 6291460
  252.2 14.9 %copy-start.4 = (f32[4096,128]{0,1:T(8,128)}, f32[4096,128]{0,1:T(8,128)S(1)}, u32[]{:S(2)}) copy-start(f32[4096,128]{0,1:T(8,128)S(1)} %fusion.26) | copy-start | bytes 6291460
  267.1 1.4 copy-start.6
  275.9 1.6 copy-start.3
  275.9 2.2 copy-start.5
  275.9 2.8 copy-start.7
  278.7 3.3 slice-start
  356.0 13.9 %copy-start.1 = (s32[1,1,4,16]{3,2,1,0:T(4,128)S(1)}, s32[1,1,4,16]{3,2,1,0:T(4,128)}, u32[]{:S(2)}) copy-start(s32[1,1,4,16]{3,2,1,0:T(4,128)} %param.7) | copy-start | bytes 772
Sparse Core Ops, SparseCore 0:
  52.8 35.3 all-reduce.3
  276.0 47.2 all-reduce.5
where the time goes:
time: 382 us; the launch traced here: 377 us
  other arithmetic  157 us (41%)
  matrix products  74.2 us (19%)
  waiting for transfers between devices  63.7 us (17%)
  local copies, waits for them, and re-layouts  48.9 us (13%)
  between operations  17.9 us (5%)
  starting transfers between devices  15.5 us (4%)
    another operation x14, other arithmetic, local(): pivot_factor = jnp.linalg.cholesky(symmetric)  78.9 us
    psum x2, waiting for transfers between devices, spread(): return lax.psum(jnp.where(mine, array, jnp.zeros_like(array)), axis)  55.9 us
    another operation x4, other arithmetic, right_solve(): lax.linalg.triangular_solve(factor, rows, left_side=False, lower=True, tr...  46.2 us
    another operation x7, matrix products, right_solve(): lax.linalg.triangular_solve(factor, rows, left_side=False, lower=True, tr...  37.5 us
    dot_general x1, matrix products, local(): jnp.dot(solved, window.T, precision=lax.Precision.HIGHEST)  32.7 us
    unnamed x26, local copies, waits for them, and re-layouts  14.5 us
    scatter-add x1, other arithmetic, local(): schur_part.at[flat_rows].add(trailing_rows.reshape(-1, win_cols))  13.9 us
    another operation x20, local copies, waits for them, and re-layouts  11.2 us
  transfers between devices with their start and end apart: 5, of which 4 were waited for; matrix products, arithmetic and copies ran while one was open for 65% of the time, Pallas kernels for 0%

commit v1 on v0

--- a/solution.py
+++ b/solution.py
@@ -9,7 +9,11 @@
 
 def spread(array, axis, root):
     mine = lax.axis_index(axis) == root
-    return lax.psum(jnp.where(mine, array, jnp.zeros_like(array)), axis)
+
+    def end_column_on(raw):
+        return jnp.sum(lax.all_gather(raw, axis), axis=0)
+
+    return end_column_on(jnp.where(mine, array, jnp.zeros_like(array)))
 
 
 def right_solve(factor, rows):

time: 382 us -> 398 us (1.042)
  waiting for transfers between devices: 63.7 us -> 72.2 us
  other arithmetic: 157 us -> 165 us
  local copies, waits for them, and re-layouts: 48.9 us -> 43.4 us
  matrix products: 74.2 us -> 78.3 us
    all_gather x0 -> x2, waiting for transfers between devices: none -> 64.2 us  [end_column_on(): return jnp.sum(lax.all_gather(raw, axis), axis=0)]
    psum x2 -> x0, waiting for transfers between devices: 55.9 us -> none  [spread(): return lax.psum(jnp.where(mine, array, jnp.zeros_like(array)), axis)]
    reduce_sum x0 -> x2, other arithmetic: none -> 8.22 us  [end_column_on(): return jnp.sum(lax.all_gather(raw, axis), axis=0)]
    another operation x1 -> x4, local copies, waits for them, and re-layouts: 0.01 us -> 8.11 us  [right_solve(): lax.linalg.triangular_solve(factor, rows, left_side=False, lower=True, tr...]
    unnamed x26 -> x24, local copies, waits for them, and re-layouts: 14.5 us -> 6.62 us
    another operation x20 -> x12, local copies, waits for them, and re-layouts: 11.2 us -> 10.3 us
  transfers between devices with their start and end apart: 5 -> 5, of which waited for: 4 -> 4; matrix products, arithmetic and copies ran while one was open for 65% -> 16% of each run, Pallas kernels for 0% -> 0%
where the time goes in v1:
time: 398 us; the launch traced here: 394 us
  other arithmetic  165 us (41%)
  matrix products  78.3 us (20%)
  waiting for transfers between devices  72.2 us (18%)
  local copies, waits for them, and re-layouts  43.4 us (11%)
  between operations  17.8 us (4%)
  starting transfers between devices  17.1 us (4%)
    another operation x14, other arithmetic, local(): pivot_factor = jnp.linalg.cholesky(symmetric)  78.8 us
    all_gather x2, waiting for transfers between devices, end_column_on(): return jnp.sum(lax.all_gather(raw, axis), axis=0)  64.2 us
    another operation x4, other arithmetic, right_solve(): lax.linalg.triangular_solve(factor, rows, left_side=False, lower=True, tr...  44.3 us
    another operation x7, matrix products, right_solve(): lax.linalg.triangular_solve(factor, rows, left_side=False, lower=True, tr...  39.9 us
    dot_general x1, matrix products, local(): jnp.dot(solved, window.T, precision=lax.Precision.HIGHEST)  32.9 us
    scatter-add x1, other arithmetic, local(): schur_part.at[flat_rows].add(trailing_rows.reshape(-1, win_cols))  13.9 us
    another operation x12, local copies, waits for them, and re-layouts  10.3 us
    scatter-add x1, other arithmetic, local(): local_rows[:, :panel_cols].at[flat_rows]  9.01 us
  transfers between devices with their start and end apart: 5, of which 4 were waited for; matrix products, arithmetic and copies ran while one was open for 16% of the time, Pallas kernels for 0%

profile of v1, /device:TPU:0, one launch (start us, length us, event | category | flops | bytes accessed | tf_op | source)
XLA Modules:
  0.0 393.9 jit_solution(2138249554151324940)
XLA Ops:
  7.2 0.9 convert_reduce_fusion
  8.1 0.7 fusion.38
  8.8 1.2 scatter_custom_fusion
  9.9 7.3 %all-to-all-start = ((s32[8,2,16]{2,1,0:T(2,128)}), s32[8,2,16]{2,1,0:T(2,128)S(1)}, u32[]{:S(2)}, u32[]{:S(2)}) async-start(s32[8,2,16]{2,1,0:T(2,128)} %bitcast.7), calls=%async_computation | async-start | bytes 16384 | tf_op jit(solution)/shard_map/all_to_all | solution.py:45
  17.2 0.9 slice.147
  18.1 0.9 broadcast_in_dim.31
  18.9 2.0 scatter_fusion
  21.0 2.7 all-to-all-done
  23.7 3.5 all-to-all-start.1
  27.9 7.8 %slice.146 = f32[4096,512]{1,0:T(8,128)} slice(f32[4096,1408]{1,0:T(8,128)} %bitcast.82), slice={[0:4096], [0:512]} | slice | bytes 16777216 | tf_op jit(solution)/shard_map/slice | solution.py:48
  35.7 5.2 %all-to-all-done.1 = f32[8,2,16,512]{3,2,1,0:T(8,128)S(1)} async-done(((f32[8,2,16,512]{3,2,1,0:T(8,128)}), f32[8,2,16,512]{3,2,1,0:T(8,128)S(1)}, u32[]{:S(2)}, u32[]{:S(2)}) %all-to-all-start.1) | async-done | bytes 524320 | tf_op jit(solution)/shard_map/all_to_all | solution.py:44
  40.9 9.0 %scatter_fusion.1 = f32[4096,512]{1,0:T(8,128)} fusion(f32[4096,512]{1,0:T(8,128)} %slice.146, s32[256]{0:T(256)S(1)} %bitcast.90, f32[256,512]{1,0:T(8,128)S(1)} %bitcast.87), kind=kCustom, calls=%fused_computation.2 | custom fusion | flops 131072 | bytes 1573888 | tf_op jit(solution)/shard_map/scatter-add | solution.py:48
  49.9 2.3 slice_select_fusion
  52.8 33.1 %all-gather.5.cloned.1.call-done = f32[2048,512]{1,0:T(8,128)} async-done(((f32[512,512]{1,0:T(8,128)}), f32[2048,512]{1,0:T(8,128)}) %all-gather.5.cloned.1.call-update) | async-done | bytes 4194320 | tf_op jit(solution)/shard_map/all_gather | solution.py:14
  85.9 2.8 reduce_sum.31
  89.3 1.0 copy-done.11
  90.3 11.7 %cholesky.103 = f32[128,128]{1,0:T(8,128)S(1)} custom-call(f32[128,128]{1,0:T(8,128)S(1)} %cholesky.263), custom_call_target="Cholesky" | custom-call | tf_op jit(solution)/shard_map/jit(cholesky)/cholesky | solution.py:57
  102.2 9.8 %custom-call.30 = f32[1,128,128]{1,2,0:T(8,128)S(1)} custom-call(f32[1,128,128]{2,1,0:T(8,128)S(1)} %get-tuple-element.29), custom_call_target="InvertDiagBlocksLowerTriangular" | custom-call | tf_op jit(solution)/shard_map/jit(cholesky)/cholesky | solution.py:57
  112.0 1.2 constant_dynamic-update-slice_fusion.3
  113.2 1.3 convolution_subtract_fusion.2
  114.5 11.7 %cholesky.215 = f32[128,128]{1,0:T(8,128)S(1)} custom-call(f32[128,128]{1,0:T(8,128)S(1)} %cholesky.267), custom_call_target="Cholesky" | custom-call | tf_op jit(solution)/shard_map/jit(cholesky)/cholesky | solution.py:57
  126.3 9.9 %custom-call.31 = f32[1,128,128]{1,2,0:T(8,128)S(1)} custom-call(f32[1,128,128]{2,1,0:T(8,128)S(1)} %get-tuple-element.26), custom_call_target="InvertDiagBlocksLowerTriangular" | custom-call | tf_op jit(solution)/shard_map/jit(cholesky)/cholesky | solution.py:57
  136.5 1.3 convolution_subtract_fusion.3
  137.8 11.7 %cholesky.236 = f32[128,128]{1,0:T(8,128)S(1)} custom-call(f32[128,128]{1,0:T(8,128)S(1)} %cholesky.272), custom_call_target="Cholesky" | custom-call | tf_op jit(solution)/shard_map/jit(cholesky)/cholesky | solution.py:57
  149.5 0.7 compare_reduce_fusion.1
  150.2 9.8 %custom-call.32 = f32[1,128,128]{1,2,0:T(8,128)S(1)} custom-call(f32[1,128,128]{2,1,0:T(8,128)S(1)} %get-tuple-element.23), custom_call_target="InvertDiagBlocksLowerTriangular" | custom-call | tf_op jit(solution)/shard_map/jit(cholesky)/cholesky | solution.py:57
  160.2 1.2 convolution_subtract_fusion.4
  161.5 11.9 %cholesky.253 = f32[128,128]{1,0:T(8,128)S(1)} custom-call(f32[128,128]{1,0:T(8,128)S(1)} %convolution_subtract_fusion.4), custom_call_target="Cholesky" | custom-call | tf_op jit(solution)/shard_map/jit(cholesky)/cholesky | solution.py:57
  173.4 0.7 compare_reduce_fusion
  174.1 0.6 compare_reduce_fusion.2
  177.4 10.4 %while.1 = (s32[]{:T(128)}, f32[512,512]{1,0:T(8,128)S(1)}, s32[4,2]{0,1:T(2,128)S(1)}, f32[4,128,128]{2,1,0:T(8,128)}, s32[]{:T(128)}) while((s32[]{:T(128)}, f32[512,512]{1,0:T(8,128)S(1)}, s32[4,2]{0,1:T(2,128)S(1)}, f32[4,128,128]{2,1,0:T(8,128)}, s32[]{:T(128)}) %tuple.31), condition=%wide.while_cond, body=%wide.while_body.sunk | while | flops 2 | bytes 132205 | solution.py:20
  178.1 2.0 bitcast_dynamic-update-slice_fusion.2
  180.7 2.0 bitcast_dynamic-update-slice_fusion.2
  183.2 2.0 bitcast_dynamic-update-slice_fusion.2
  185.8 2.0 bitcast_dynamic-update-slice_fusion.2
  187.8 1.0 copy-done.10
  188.8 40.1 %custom-call.33 = f32[4,128,128]{1,2,0:T(8,128)S(1)} custom-call(f32[4,128,128]{2,1,0:T(8,128)} %get-tuple-element.9), custom_call_target="InvertDiagBlocksLowerTriangular" | custom-call | tf_op jit(solution)/shard_map/triangular_solve | solution.py:20
  228.9 3.6 fusion.12
  232.5 1.9 copy.18
  234.4 5.2 %convolution_subtract_fusion.1 = f32[4096,128]{1,0:T(8,128)S(1)} fusion(f32[4096,128]{0,1:T(8,128)S(1)} %fusion.12, f32[4096,512]{1,0:T(8,128)} %scatter_fusion.1, f32[512,512]{1,0:T(8,128)} %copy-done.10), kind=kOutput, calls=%fused_computation.17 | convolution fusion | flops 805830656 | bytes 6356992 | tf_op jit(solution)/shard_map/triangular_solve | solution.py:20
  239.5 3.3 fusion.27
  242.9 3.4 copy.19
  246.2 9.4 %convolution_subtract_fusion = f32[4096,128]{1,0:T(8,128)S(1)} fusion(f32[4096,128]{0,1:T(8,128)} %fusion.27, f32[4096,128]{0,1:T(8,128)S(1)} %fusion.12, f32[4096,512]{1,0:T(8,128)} %scatter_fusion.1, f32[512,512]{1,0:T(8,128)} %copy-done.10), kind=kOutput, calls=%fused_computation.16 | convolution fusion | flops 1612185600 | bytes 8519680 | tf_op jit(solution)/shard_map/triangular_solve | solution.py:20
  255.7 2.0 fusion.26
  257.7 1.3 copy-done.9
  259.0 12.9 %fusion.6 = f32[4096,128]{1,0:T(8,128)} fusion(f32[4096,128]{0,1:T(8,128)S(1)} %fusion.26, f32[4096,128]{0,1:T(8,128)S(1)} %copy-done.8, f32[4096,128]{0,1:T(8,128)S(1)} %fusion.12, f32[4096,512]{1,0:T(8,128)} %scatter_fusion.1, f32[512,512]{1,0:T(8,128)} %copy-done.10), kind=kOutput, calls=%fused_computation.18 | convolution fusion | flops 2419589120 | bytes 10682368 | tf_op jit(solution)/shard_map/triangular_solve | solution.py:20
  271.9 2.9 copy.20
  274.8 3.5 fusion.25
  278.3 1.4 copy-done.6
  279.7 2.4 maximum_select_fusion
  282.2 1.0 slice.151
  283.1 1.0 broadcast_in_dim.35
  284.1 2.2 scatter_fusion.2
  286.3 5.8 %all-to-all-start.2 = ((f32[8,2,16,896]{3,2,1,0:T(8,128)}), f32[8,2,16,896]{3,2,1,0:T(8,128)}, u32[]{:S(2)}, u32[]{:S(2)}) async-start(f32[8,2,16,896]{3,2,1,0:T(8,128)} %bitcast.85), calls=%async_computation.2 | async-start | bytes 1835008 | tf_op jit(solution)/shard_map/all_to_all | solution.py:51
  292.1 4.0 %pad_maximum_fusion = f32[4096,512]{1,0:T(8,128)S(1)} fusion(f32[4096,128]{1,0:T(8,128)} %copy-done.6, f32[4096,128]{1,0:T(8,128)} %copy.20, f32[4096,128]{1,0:T(8,128)} %copy.19, f32[4096,128]{1,0:T(8,128)S(1)} %copy-done.2), kind=kLoop, calls=%fused_computation.8 | loop fusion | flops 6291456 | bytes 16777216 | tf_op jit(solution)/shard_map/triangular_solve | solution.py:20
  296.2 0.9 slice.149
  297.1 0.7 copy-done.4
  297.7 0.6 copy-done.5
  298.4 0.6 copy-done.7
  299.2 4.4 %maximum_bitcast_fusion = f32[1,4096,512]{2,1,0:T(8,128)} fusion(f32[3584,512]{1,0:T(8,128)S(1)} %slice.149, f32[512,512]{1,0:T(8,128)S(1)} %maximum_select_fusion.1), kind=kLoop, calls=%fused_computation.9 | loop fusion | flops 2097152 | bytes 16777216 | tf_op jit(solution)/shard_map/broadcast_in_dim | solution.py:66
  303.5 31.1 %all-gather.7.cloned.1.call-done = f32[3584,512]{1,0:T(8,128)} async-done(((f32[896,512]{1,0:T(8,128)}), f32[3584,512]{1,0:T(8,128)}) %all-gather.7.cloned.1.call-update) | async-done | bytes 7340048 | tf_op jit(solution)/shard_map/all_gather | solution.py:14
  334.7 5.4 %reduce_sum.32 = f32[896,512]{1,0:T(8,128)} reduce(f32[4,896,512]{2,1,0:T(8,128)} %bitcast.84, f32[]{:T(128)} %constant.157.clone.1), dimensions={0}, to_apply=%region_13.14 | reduce | flops 1376256 | bytes 9175044 | tf_op jit(solution)/shard_map/reduce_sum | solution.py:14
  340.1 32.9 %slice_subtract_fusion = f32[4096,896]{1,0:T(8,128)} fusion(f32[4096,1408]{1,0:T(8,128)} %bitcast.83, f32[896,512]{1,0:T(8,128)} %reduce_sum.32, f32[4096,128]{1,0:T(8,128)} %copy-done.6, f32[4096,128]{1,0:T(8,128)} %copy.20, f32[4096,128]{1,0:T(8,128)} %copy.19, f32[4096,128]{1,0:T(8,128)S(1)} %copy-done.2), kind=kOutput, calls=%fused_computation.7 | convolution fusion | flops 22558539776 | bytes 39583744 | tf_op jit(solution)/shard_map/dot_general | solution.py:60
  373.0 13.9 %scatter_fusion.3 = f32[4096,896]{1,0:T(8,128)} fusion(f32[4096,896]{1,0:T(8,128)} %slice_subtract_fusion, s32[256]{0:T(256)S(1)} %bitcast.91, f32[256,896]{1,0:T(8,128)} %bitcast.27), kind=kCustom, calls=%fused_computation.4 | custom fusion | flops 229376 | bytes 2753536 | tf_op jit(solution)/shard_map/scatter-add | solution.py:63
  (49 shorter events, 4.8 us)
Async XLA Ops:
  7.2 1.6 copy-start
  9.9 13.8 %all-to-all-start = ((s32[8,2,16]{2,1,0:T(2,128)}), s32[8,2,16]{2,1,0:T(2,128)S(1)}, u32[]{:S(2)}, u32[]{:S(2)}) async-start(s32[8,2,16]{2,1,0:T(2,128)} %bitcast.7), calls=%async_computation | async-start | bytes 16384 | tf_op jit(solution)/shard_map/all_to_all | solution.py:45
  23.7 17.2 %all-to-all-start.1 = ((f32[8,2,16,512]{3,2,1,0:T(8,128)}), f32[8,2,16,512]{3,2,1,0:T(8,128)S(1)}, u32[]{:S(2)}, u32[]{:S(2)}) async-start(f32[8,2,16,512]{3,2,1,0:T(8,128)} %bitcast.10), calls=%async_computation.1 | async-start | bytes 1048576 | tf_op jit(solution)/shard_map/all_to_all | solution.py:44
  27.2 58.7 %all-gather.5.cloned.1.call-start = ((), (), s32[]{:S(2)}) async-start(), calls=%async_computation.3 | async-start | bytes 5242880 | tf_op jit(solution)/shard_map/all_gather | solution.py:14
  52.3 282.4 %all-gather.7.cloned.1.call-start = ((), (), s32[]{:S(2)}) async-start(), calls=%async_computation.4 | async-start | bytes 9175040 | tf_op jit(solution)/shard_map/all_gather | solution.py:14
  89.3 1.0 copy-start.11
  187.8 1.0 copy-start.10
  255.7 3.3 copy-start.8
  257.7 1.3 copy-start.9
  274.8 5.0 %copy-start.2 = (f32[4096,128]{1,0:T(8,128)S(1)}, f32[4096,128]{1,0:T(8,128)}, u32[]{:S(2)}) copy-start(f32[4096,128]{1,0:T(8,128)} %copy.18) | copy-start | bytes 6291460
  274.8 5.0 %copy-start.3 = (f32[4096,128]{1,0:T(8,128)S(1)}, f32[4096,128]{1,0:T(8,128)}, u32[]{:S(2)}) copy-start(f32[4096,128]{1,0:T(8,128)} %copy.19) | copy-start | bytes 6291460
  278.3 1.4 copy-start.6
  286.3 86.7 %all-to-all-start.2 = ((f32[8,2,16,896]{3,2,1,0:T(8,128)}), f32[8,2,16,896]{3,2,1,0:T(8,128)}, u32[]{:S(2)}, u32[]{:S(2)}) async-start(f32[8,2,16,896]{3,2,1,0:T(8,128)} %bitcast.85), calls=%async_computation.2 | async-start | bytes 1835008 | tf_op jit(solution)/shard_map/all_to_all | solution.py:51
  296.1 1.6 copy-start.4
  296.1 2.2 copy-start.5
  296.2 2.8 copy-start.7
  373.0 13.9 %copy-start.1 = (s32[1,1,4,16]{3,2,1,0:T(4,128)S(1)}, s32[1,1,4,16]{3,2,1,0:T(4,128)}, u32[]{:S(2)}) copy-start(s32[1,1,4,16]{3,2,1,0:T(4,128)} %param.7) | copy-start | bytes 772
Sparse Core Ops, SparseCore 0:
  52.4 33.5 all-gather.4
  282.3 52.3 all-gather.6
